TPU v7x, 32 devices: a whole 2x2x4 slice. The times are simulated.
32 devices in a mesh: group: 2 (over x), seq: 8 (over z, y), dp: 2 (over core).
Axes of the slice: x: 2, y: 2, z: 4, core: 2. Of those that a mesh axis runs over, the one named last changes fastest.
Arguments:
- queries: bfloat16 [4, 1024, 512], P(('group', 'dp'), 'seq'), parts along dimension 0, may hold values from -6 to 6
- key_rows: bfloat16 [4, 1024, 512], P(('group', 'dp'), 'seq'), parts along dimension 0, may hold values from -6 to 6
- value_rows: bfloat16 [4, 1024, 768], P(('group', 'dp'), 'seq'), parts along dimension 0, may hold values from -6 to 6
- trunk_state: bfloat16 [4, 1024, 768], P(('group', 'dp'), 'seq'), parts along dimension 0, may hold values from -6 to 6
- skip_input: bfloat16 [4, 2048, 768], P(('group', 'dp'), 'seq'), parts along dimension 0, may hold values from -6 to 6
- norm_gain: bfloat16 [768], replicated, may hold values from 0.099609375 to 1.8984375
- conv_weight: bfloat16 [3840, 384], replicated, may hold values from -0.09375 to 0.09375
- cotangent: bfloat16 [4, 2048, 384], P(('group', 'dp'), 'seq'), parts along dimension 0, may hold values from -6 to 6
Outputs:
- decoded: bfloat16 [4, 2048, 384], P(('group', 'dp'), 'seq'), parts along dimension 0
- grad_queries: bfloat16 [4, 1024, 512], P(('group', 'dp'), 'seq'), parts along dimension 0
- grad_keys: bfloat16 [4, 1024, 512], P(('group', 'dp'), 'seq'), parts along dimension 0
- grad_values: bfloat16 [4, 1024, 768], P(('group', 'dp'), 'seq'), parts along dimension 0
- grad_trunk: bfloat16 [4, 1024, 768], P(('group', 'dp'), 'seq'), parts along dimension 0
- grad_skip: bfloat16 [4, 2048, 768], P(('group', 'dp'), 'seq'), parts along dimension 0
- grad_weight: float32 [7680, 384], P(('group', 'seq', 'dp')), parts along dimension 0
There are 2 independent parts, one for each index of `group`. A program takes and returns all parts, laid end to end along the dimension named above; an argument that names none is the same for every part. Nothing has to cross between parts.
All inputs are finite; a program needn't handle non-finite values.
Results may differ from a plain program's by a relative error of at most 0.029.
Values may be sent and summed in bfloat16 or wider, within the bound.
No kernel may reach another device: no remote copies, remote signals or barrier semaphores. Data moves between devices by JAX's collectives and lax.ppermute only.
A program may use at most 128 MiB of HBM per device.

v0:
```python
import math
import jax
import jax.numpy as jnp
from jax import lax
from jax.sharding import PartitionSpec as P

H = 4
DK = 128
DV = 192
C = 768
CO = 384
KW = 5


def extended(array, sides, width):
    for axis, dim in sides:
        count, length = (lax.axis_size(axis), array.shape[dim])
        up = [(i, (i + 1) % count) for i in range(count - 1)]
        down = [(j, i) for i, j in up]
        last = lax.slice_in_dim(array, length - width, length, axis=dim)
        initial = lax.slice_in_dim(array, 0, width, axis=dim)
        before = lax.ppermute(last, axis, up)
        after = lax.ppermute(initial, axis, down)
        array = jnp.concatenate([before, array, after], axis=dim)
    return array


def gelu_parts(preact):
    cdf_value = 0.5 * (1.0 + jax.scipy.special.erf(preact * (1.0 / math.sqrt(2.0))))
    density = jnp.exp(-0.5 * preact * preact) * (1.0 / math.sqrt(2.0 * math.pi))
    return (preact * cdf_value, cdf_value + preact * density)


def window_rows(padded, kernel, row_count):
    return jnp.concatenate(
        [padded[offset : offset + row_count] for offset in range(kernel)], axis=1
    )


def body(queries, key_rows, value_rows, trunk_state, skip_input, norm_gain, conv_weight, cotangent):
    score_scale = DK ** (-0.5)
    local_tokens = queries.shape[1]
    positions = 2 * local_tokens
    half_kernel = KW // 2
    query_heads = queries[0].reshape(local_tokens, H, DK)
    gathered = (
        lax.all_gather(key_rows, "seq", axis=1, tiled=True),
        lax.all_gather(value_rows, "seq", axis=1, tiled=True),
    )
    all_keys = gathered[0][0].reshape(-1, H, DK)
    all_values = gathered[1][0].reshape(-1, H, DV)
    scores = (
        jnp.einsum("ihd,jhd->hij", query_heads, all_keys, preferred_element_type=jnp.float32)
        * score_scale
    )
    row_peak = jnp.max(scores, axis=2, keepdims=True)
    row_total = jnp.sum(jnp.exp(scores - row_peak), axis=2, keepdims=True)
    logsum = row_peak + jnp.log(row_total)
    softmax = jnp.exp(scores - logsum)
    rounded = softmax.astype(jnp.bfloat16)
    attended = jnp.einsum(
        "hij,jhd->ihd", rounded, all_values, preferred_element_type=jnp.float32
    ).astype(jnp.bfloat16)
    hidden = trunk_state[0].astype(jnp.float32) + attended.reshape(local_tokens, H * DV).astype(
        jnp.float32
    )
    merged = jnp.repeat(hidden, 2, axis=0) + skip_input[0].astype(jnp.float32)
    inverse = lax.rsqrt(jnp.mean(merged * merged, axis=1, keepdims=True) + 1e-06)
    channel_gain = norm_gain.astype(jnp.float32)
    normed = (merged * inverse * channel_gain).astype(jnp.bfloat16)
    padded = extended(normed, (("seq", 0),), half_kernel)
    columns = window_rows(padded, KW, positions)
    preact = jnp.dot(columns, conv_weight, preferred_element_type=jnp.float32)
    activated, derivative = gelu_parts(preact)
    decoded = activated.astype(jnp.bfloat16)
    grad_pre = (cotangent[0].astype(jnp.float32) * derivative).astype(jnp.bfloat16)
    grad_padded = extended(grad_pre, (("seq", 0),), half_kernel)
    norm_scale = (lax.axis_size("dp") * positions * lax.axis_size("seq")) ** (-0.5)
    grad_weight = lax.psum_scatter(
        lax.dot_general(
            columns, grad_pre, (((0,), (0,)), ((), ())), preferred_element_type=jnp.float32
        )
        * norm_scale,
        ("seq", "dp"),
        scatter_dimension=0,
        tiled=True,
    )
    stacked = jnp.stack(
        [
            grad_padded[2 * half_kernel - offset : 2 * half_kernel - offset + positions]
            for offset in range(KW)
        ],
        axis=1,
    )
    weight_blocks = conv_weight.reshape(KW, C, CO)
    grad_normed = jnp.einsum(
        "pko,kco->pc", stacked, weight_blocks, preferred_element_type=jnp.float32
    )
    scaled_grad = grad_normed * channel_gain
    grad_merged = inverse * scaled_grad - merged * inverse**3 * jnp.mean(
        scaled_grad * merged, axis=1, keepdims=True
    )
    grad_skip = grad_merged.astype(jnp.bfloat16)
    grad_trunk = grad_merged.reshape(local_tokens, 2, C).sum(axis=1).astype(jnp.bfloat16)
    grad_heads = grad_trunk.reshape(local_tokens, H, DV)
    row_delta = jnp.sum(grad_heads.astype(jnp.float32) * attended.astype(jnp.float32), axis=2)
    value_grad = jnp.einsum(
        "ihd,jhd->hij", grad_heads, all_values, preferred_element_type=jnp.float32
    )
    slopes = (softmax * (value_grad - row_delta.T[:, :, None])).astype(jnp.bfloat16)
    grad_queries = (
        jnp.einsum("hij,jhd->ihd", slopes, all_keys, preferred_element_type=jnp.float32)
        * score_scale
    ).astype(jnp.bfloat16)
    key_part = (
        jnp.einsum("hij,ihd->jhd", slopes, query_heads, preferred_element_type=jnp.float32)
        * score_scale
    )
    value_part = jnp.einsum("hij,ihd->jhd", rounded, grad_heads, preferred_element_type=jnp.float32)
    summed = lax.psum_scatter(
        jnp.concatenate(
            [
                key_part.reshape(lax.axis_size("seq") * local_tokens, H * DK),
                value_part.reshape(lax.axis_size("seq") * local_tokens, H * DV),
            ],
            axis=1,
        ).astype(jnp.bfloat16),
        "seq",
        scatter_dimension=0,
        tiled=True,
    ).astype(jnp.float32)
    grad_keys = summed[:, : H * DK].astype(jnp.bfloat16)
    grad_values = summed[:, H * DK :].astype(jnp.bfloat16)
    return (
        decoded[None],
        grad_queries.reshape(local_tokens, H * DK)[None],
        grad_keys[None],
        grad_values[None],
        grad_trunk[None],
        grad_skip[None],
        grad_weight,
    )


def solution(mesh):
    return jax.shard_map(
        body,
        mesh=mesh,
        in_specs=(
            P(("group", "dp"), "seq", None),
            P(("group", "dp"), "seq", None),
            P(("group", "dp"), "seq", None),
            P(("group", "dp"), "seq", None),
            P(("group", "dp"), "seq", None),
            P(),
            P(),
            P(("group", "dp"), "seq", None),
        ),
        out_specs=(
            P(("group", "dp"), "seq", None),
            P(("group", "dp"), "seq", None),
            P(("group", "dp"), "seq", None),
            P(("group", "dp"), "seq", None),
            P(("group", "dp"), "seq", None),
            P(("group", "dp"), "seq", None),
            P(("group", "seq", "dp"), None),
        ),
        check_vma=False,
    )
```

profile of v0, /device:TPU:0, one launch (start us, length us, event | category | flops | bytes accessed | tf_op | source)
XLA Modules:
  0.0 324.4 jit_solution(8928119127070148307)
XLA Ops:
  7.2 0.0 copy-start
  7.2 0.0 all-gather.3.cloned.1.call-start
  7.2 1.8 copy.24
  9.0 0.0 all-gather.3.cloned.1.call-update
  9.1 0.0 all-gather.5.cloned.1.call-start
  9.1 0.7 all-gather.5.cloned.1.call-update
  9.8 0.0 reduce-scatter.3.cloned.1.call-start
  9.9 0.7 convert_element_type.100
  10.6 1.0 copy.35
  11.6 0.0 copy-start.11
  11.6 41.2 %all-gather.3.cloned.1.call-done = bf16[1,1024,512]{1,2,0:T(8,128)(2,1)} async-done(((bf16[1,128,512]{1,2,0:T(8,128)(2,1)}), bf16[1,1024,512]{1,2,0:T(8,128)(2,1)}) %all-gather.3.cloned.1.call-update) | async-done | bytes 1048592 | tf_op jit(solution)/shard_map/all_gather | solution.py:47
  52.8 1.8 multiply_reduce_fusion
  54.6 1.3 copy-done.1
  55.9 0.5 exponential_reduce_fusion
  56.4 41.8 %all-gather.5.cloned.1.call-done = bf16[1,1024,768]{2,1,0:T(8,128)(2,1)} async-done(((bf16[1,128,768]{2,1,0:T(8,128)(2,1)}), bf16[1,1024,768]{2,1,0:T(8,128)(2,1)}) %all-gather.5.cloned.1.call-update) | async-done | bytes 1572880 | tf_op jit(solution)/shard_map/all_gather | solution.py:48
  98.2 2.6 copy.27
  100.8 2.8 fusion.2
  103.5 0.9 copy.28
  104.5 1.0 convert_add_fusion.1
  105.5 1.2 broadcast_in_dim.12
  106.7 2.6 reshape.93
  109.2 2.6 broadcast_in_dim.26
  111.8 1.3 fusion.6
  113.2 1.3 multiply_convert_fusion.2
  114.4 0.0 copy-start.14
  114.5 2.6 collective-permute-start
  117.1 1.3 collective-permute-start.1
  118.4 0.1 fusion.10
  118.5 0.1 fusion.18
  118.6 4.3 %collective-permute-done.1 = bf16[2,768]{1,0:T(2,128)(2,1)S(1)} collective-permute-done((bf16[2,768]{1,0:T(2,128)(2,1)S(1)}, bf16[2,768]{1,0:T(2,128)(2,1)S(1)}, u32[]{:S(2)}, u32[]{:S(2)}) %collective-permute-start.1) | collective-permute-done | bytes 3104 | tf_op jit(solution)/shard_map/ppermute | solution.py:23
  122.9 0.1 fusion.8
  123.0 0.1 fusion.17
  123.1 2.0 fusion.16
  125.2 1.4 collective-permute-start.2
  126.6 5.4 %collective-permute-start.3 = (bf16[2,384]{1,0:T(2,128)(2,1)S(1)}, bf16[2,384]{1,0:T(2,128)(2,1)S(1)}, u32[]{:S(2)}, u32[]{:S(2)}) collective-permute-start(bf16[2,384]{1,0:T(2,128)(2,1)S(1)} %get-tuple-element.27), channel_id=1, source_target_pairs={{0,2},{2,4},{4,6},{6,8},{8,10},{10,12},{12,14},{1,3},{3,5},{5,7},{... | collective-permute-start | bytes 4616 | tf_op jit(solution)/shard_map/ppermute | solution.py:22
  132.1 0.1 fusion.25
  132.1 0.1 fusion.30
  132.2 1.1 collective-permute-done.3
  133.3 0.1 fusion.22
  133.4 0.1 fusion.28
  133.5 1.1 multiply_reduce_fusion.1
  134.6 1.3 convert_bitcast_fusion.1
  135.9 2.5 reshape.95
  138.4 2.8 reduce_sum.48
  141.2 1.7 copy.29
  142.9 1.1 fusion.19
  144.1 3.6 %convolution_convert_fusion = bf16[4,192,1024]{2,1,0:T(8,128)(2,1)} fusion(bf16[128,4,192]{0,2,1:T(8,128)(2,1)} %bitcast.94, f32[4,128,1024]{2,1,0:T(8,128)} %copy-done.1, f32[4,128]{1,0:T(4,128)S(1)} %log_add_fusion), kind=kOutput, calls=%fused_computation.8 | convolution fusion | flops 203685888 | bytes 3868672 | tf_op jit(solution)/shard_map/hij,ihd->jhd/dot_general | solution.py:119
  147.7 0.0 copy-start.12
  147.7 0.8 multiply_convert_fusion.1
  148.6 1.0 copy-done.5
  149.6 1.4 multiply_convert_fusion
  151.0 2.3 copy.31
  153.2 2.6 copy.32
  155.9 3.4 %pad_maximum_fusion = bf16[1024,1280]{1,0:T(8,128)(2,1)} fusion(bf16[1024,768]{1,0:T(8,128)(2,1)} %copy.32, bf16[1024,512]{1,0:T(8,128)(2,1)} %copy.31), kind=kLoop, calls=%fused_computation.1 | loop fusion | flops 5242880 | bytes 5242880 | tf_op jit(solution)/shard_map/concatenate | solution.py:121
  159.3 0.0 reduce-scatter.3.cloned.1.call-update
  159.3 0.0 reduce-scatter.5.cloned.1.call-start
  159.3 5.3 %convolution_multiply_fusion = f32[3840,384]{1,0:T(8,128)} fusion(bf16[256,3840]{1,0:T(8,128)(2,1)} %copy-done.7, bf16[256,384]{1,0:T(8,128)(2,1)S(1)} %get-tuple-element.23), kind=kOutput, calls=%fused_computation | convolution fusion | flops 756449280 | bytes 8060928 | tf_op jit(solution)/shard_map/dot_general | solution.py:80
  164.6 0.0 reduce-scatter.5.cloned.1.call-update
  164.7 2.0 fusion.3
  166.6 0.8 copy.33
  167.4 64.6 %reduce-scatter.3.cloned.1.call-done = bf16[128,1280]{1,0:T(8,128)(2,1)} async-done(((bf16[1024,1280]{1,0:T(8,128)(2,1)}), bf16[128,1280]{1,0:T(8,128)(2,1)}) %reduce-scatter.3.cloned.1.call-update) | async-done | bytes 327696 | tf_op jit(solution)/shard_map/reduce_scatter | solution.py:120
  232.0 1.6 slice_bitcast_fusion.1
  233.6 1.6 slice_bitcast_fusion
  235.2 82.7 %reduce-scatter.5.cloned.1.call-done = f32[240,384]{1,0:T(8,128)} async-done(((f32[3840,384]{1,0:T(8,128)}), f32[240,384]{1,0:T(8,128)}) %reduce-scatter.5.cloned.1.call-update) | async-done | bytes 368656 | tf_op jit(solution)/shard_map/reduce_scatter | solution.py:79
  (33 shorter events, 0.2 us)
Async XLA Ops:
  7.2 115.9 %copy-start = (bf16[3840,384]{1,0:T(8,128)(2,1)S(1)}, bf16[3840,384]{1,0:T(8,128)(2,1)}, u32[]{:S(2)}) copy-start(bf16[3840,384]{1,0:T(8,128)(2,1)} %param.14) | copy-start | bytes 8847364
  7.2 45.6 %all-gather.3.cloned.1.call-start = ((), (), s32[]{:S(2)}) async-start(), calls=%async_computation.2 | async-start | bytes 1179648 | tf_op jit(solution)/shard_map/all_gather | solution.py:47
  9.1 89.1 %all-gather.5.cloned.1.call-start = ((), (), s32[]{:S(2)}) async-start(), calls=%async_computation.3 | async-start | bytes 1769472 | tf_op jit(solution)/shard_map/all_gather | solution.py:48
  9.8 222.2 %reduce-scatter.3.cloned.1.call-start = ((), (), s32[]{:S(2)}) async-start(), calls=%async_computation.4 | async-start | bytes 2949120 | tf_op jit(solution)/shard_map/reduce_scatter | solution.py:120
  11.6 44.8 %copy-start.11 = (bf16[1,128,512]{1,2,0:T(8,128)(2,1)}, bf16[1,128,512]{1,2,0:T(8,128)(2,1)S(1)}, u32[]{:S(2)}) copy-start(bf16[1,128,512]{1,2,0:T(8,128)(2,1)S(1)} %copy.35) | copy-start | bytes 393220
  54.5 1.3 copy-start.1
  100.8 3.7 %copy-start.13 = (bf16[1,128,768]{2,1,0:T(8,128)(2,1)S(1)}, bf16[1,128,768]{2,1,0:T(8,128)(2,1)}, u32[]{:S(2)}) copy-start(bf16[1,128,768]{2,1,0:T(8,128)(2,1)} %param.11) | copy-start | bytes 589828
  103.5 0.9 copy-start.8
  105.5 6.3 %copy-start.6 = (bf16[1,256,768]{2,1,0:T(8,128)(2,1)S(1)}, bf16[1,256,768]{2,1,0:T(8,128)(2,1)}, u32[]{:S(2)}) copy-start(bf16[1,256,768]{2,1,0:T(8,128)(2,1)} %param.12) | copy-start | bytes 1179652
  114.4 8.7 %copy-start.14 = (bf16[1,256,384]{2,1,0:T(8,128)(2,1)S(1)}, bf16[1,256,384]{2,1,0:T(8,128)(2,1)}, u32[]{:S(2)}) copy-start(bf16[1,256,384]{2,1,0:T(8,128)(2,1)} %param.15) | copy-start | bytes 589828
  114.5 3.9 %collective-permute-start = (bf16[2,768]{1,0:T(2,128)(2,1)S(1)}, bf16[2,768]{1,0:T(2,128)(2,1)S(1)}, u32[]{:S(2)}, u32[]{:S(2)}) collective-permute-start(bf16[2,768]{1,0:T(2,128)(2,1)S(1)} %get-tuple-element.26), channel_id=1, source_target_pairs={{0,2},{2,4},{4,6},{6,8},{8,10},{10,12},{12,14},{1,3},{3,5},{5,7},{... | collective-permute-start | bytes 9224 | tf_op jit(solution)/shard_map/ppermute | solution.py:22
  117.1 5.8 %collective-permute-start.1 = (bf16[2,768]{1,0:T(2,128)(2,1)S(1)}, bf16[2,768]{1,0:T(2,128)(2,1)S(1)}, u32[]{:S(2)}, u32[]{:S(2)}) collective-permute-start(bf16[2,768]{1,0:T(2,128)(2,1)S(1)} %get-tuple-element.25), channel_id=1, source_target_pairs={{2,0},{4,2},{6,4},{8,6},{10,8},{12,10},{14,12},{3,1},{5,3},{7,5},{... | collective-permute-start | bytes 9224 | tf_op jit(solution)/shard_map/ppermute | solution.py:23
  123.1 2.0 copy-start.7
  125.1 8.3 %copy-start.4 = (f32[256,768]{1,0:T(8,128)S(1)}, f32[256,768]{1,0:T(8,128)}, u32[]{:S(2)}) copy-start(f32[256,768]{1,0:T(8,128)} %reshape.93) | copy-start | bytes 2359300
  125.2 6.9 %collective-permute-start.2 = (bf16[2,384]{1,0:T(2,128)(2,1)S(1)}, bf16[2,384]{1,0:T(2,128)(2,1)S(1)}, u32[]{:S(2)}, u32[]{:S(2)}) collective-permute-start(bf16[2,384]{1,0:T(2,128)(2,1)S(1)} %get-tuple-element.28), channel_id=1, source_target_pairs={{2,0},{4,2},{6,4},{8,6},{10,8},{12,10},{14,12},{3,1},{5,3},{7,5},{... | collective-permute-start | bytes 4616 | tf_op jit(solution)/shard_map/ppermute | solution.py:23
  126.6 6.7 %collective-permute-start.3 = (bf16[2,384]{1,0:T(2,128)(2,1)S(1)}, bf16[2,384]{1,0:T(2,128)(2,1)S(1)}, u32[]{:S(2)}, u32[]{:S(2)}) collective-permute-start(bf16[2,384]{1,0:T(2,128)(2,1)S(1)} %get-tuple-element.27), channel_id=1, source_target_pairs={{0,2},{2,4},{4,6},{6,8},{8,10},{10,12},{12,14},{1,3},{3,5},{5,7},{... | collective-permute-start | bytes 4616 | tf_op jit(solution)/shard_map/ppermute | solution.py:22
  135.9 7.0 %copy-start.9 = (f32[4,128,192]{1,2,0:T(8,128)S(1)}, f32[4,128,192]{1,2,0:T(8,128)}, u32[]{:S(2)}) copy-start(f32[4,128,192]{1,2,0:T(8,128)} %copy-done.8) | copy-start | bytes 1179652
  142.9 4.8 %copy-start.2 = (f32[4,128,1024]{2,1,0:T(8,128)S(1)}, f32[4,128,1024]{2,1,0:T(8,128)}, u32[]{:S(2)}) copy-start(f32[4,128,1024]{2,1,0:T(8,128)} %copy-done.1) | copy-start | bytes 6291460
  142.9 4.8 %copy-start.3 = (bf16[1,1024,768]{1,2,0:T(8,128)(2,1)S(1)}, bf16[1,1024,768]{1,2,0:T(8,128)(2,1)}, u32[]{:S(2)}) copy-start(bf16[1,1024,768]{1,2,0:T(8,128)(2,1)} %copy.27) | copy-start | bytes 4718596
  142.9 4.8 %copy-start.10 = (bf16[128,768]{0,1:T(8,128)(2,1)S(1)}, bf16[128,768]{0,1:T(8,128)(2,1)}, u32[]{:S(2)}) copy-start(bf16[128,768]{0,1:T(8,128)(2,1)} %copy.29) | copy-start | bytes 589828
  147.7 1.9 copy-start.12
  148.6 1.0 copy-start.5
  159.3 158.6 %reduce-scatter.5.cloned.1.call-start = ((), (), s32[]{:S(2)}) async-start(), calls=%async_computation.5 | async-start | bytes 6266880 | tf_op jit(solution)/shard_map/reduce_scatter | solution.py:79
Sparse Core Ops, SparseCore 0:
  10.6 42.1 all-gather.2
  54.9 43.1 all-gather.4
  159.4 72.5 reduce-scatter.2
  236.4 81.4 reduce-scatter.4
where the time goes:
time: 325 us; the launch traced here: 324 us
  waiting for transfers between devices  236 us (73%)
  local copies, waits for them, and re-layouts  28.3 us (9%)
  matrix products  20.8 us (6%)
  other arithmetic  14 us (4%)
  between operations  14 us (4%)
  starting transfers between devices  10.9 us (3%)
    reduce_scatter x1, waiting for transfers between devices, body(): lax.psum_scatter(lax.dot_general(columns, grad_pre, (((0,), (0,)), ((), (...  82.7 us
    reduce_scatter x1, waiting for transfers between devices, body(): lax.psum_scatter(jnp.concatenate([key_part.reshape(lax.axis_size('seq') *...  64.6 us
    all_gather x1, waiting for transfers between devices, body(): lax.all_gather(value_rows, 'seq', axis=1, tiled=True)  41.8 us
    all_gather x1, waiting for transfers between devices, body(): lax.all_gather(key_rows, 'seq', axis=1, tiled=True)  41.2 us
    ppermute x2, starting transfers between devices, extended(): before = lax.ppermute(last, axis, up)  8.03 us
  transfers between devices with their start and end apart: 8, of which 6 were waited for; matrix products, arithmetic and copies ran while one was open for 5% of the time, Pallas kernels for 0%

commit v1 on v0

--- a/solution.py
+++ b/solution.py
@@ -10,6 +10,28 @@
 C = 768
 CO = 384
 KW = 5
+
+
+def in_order(pieces, dim):
+    pieces = jnp.moveaxis(pieces, 0, dim)
+    shape = pieces.shape
+    return pieces.reshape(*shape[:dim], shape[dim] * shape[dim + 1], *shape[dim + 2 :])
+
+
+def doubled(value, axis):
+    devices = lax.axis_size(axis)
+    pieces = value[None]
+    for level in range(devices.bit_length() - 1):
+        bit = 1 << level
+        other = lax.ppermute(pieces, axis, [(i, i ^ bit) for i in range(devices)])
+        both = jnp.stack([pieces, other])
+        upper = lax.axis_index(axis) >> level & 1
+        pieces = jnp.where(upper == 0, both, both[::-1]).reshape(-1, *value.shape)
+    return pieces
+
+
+def gather_by_bits(array, axis, dim):
+    return in_order(doubled(array, axis), dim)
 
 
 def extended(array, sides, width):
@@ -45,7 +67,7 @@
     query_heads = queries[0].reshape(local_tokens, H, DK)
     gathered = (
         lax.all_gather(key_rows, "seq", axis=1, tiled=True),
-        lax.all_gather(value_rows, "seq", axis=1, tiled=True),
+        gather_by_bits(value_rows, "seq", 1),
     )
     all_keys = gathered[0][0].reshape(-1, H, DK)
     all_values = gathered[1][0].reshape(-1, H, DV)

time: 325 us -> 309 us (0.951)
  waiting for transfers between devices: 236 us -> 206 us
  starting transfers between devices: 10.9 us -> 18.8 us
  other arithmetic: 14 us -> 20.2 us
    ppermute x0 -> x3, waiting for transfers between devices: none -> 53.6 us  [doubled(): other = lax.ppermute(pieces, axis, [(i, i ^ bit) for i in range(devices)])]
    all_gather x1 -> x0, waiting for transfers between devices: 41.8 us -> none  [body(): lax.all_gather(value_rows, 'seq', axis=1, tiled=True)]
    all_gather x1, waiting for transfers between devices: 41.2 us -> 0.01 us  [body(): lax.all_gather(key_rows, 'seq', axis=1, tiled=True)]
    ppermute x0 -> x3, starting transfers between devices: none -> 7.39 us  [doubled(): other = lax.ppermute(pieces, axis, [(i, i ^ bit) for i in range(devices)])]
    another operation x0 -> x4, other arithmetic: none -> 4.38 us  [doubled(): both = jnp.stack([pieces, other])]
    select_n x0 -> x1, local copies, waits for them, and re-layouts: none -> 3.81 us  [doubled(): pieces = jnp.where(upper == 0, both, both[::-1]).reshape(-1, *value.shape)]
    another operation x0 -> x1, local copies, waits for them, and re-layouts: none -> 3.79 us  [body(): all_values = gathered[1][0].reshape(-1, H, DV)]
  transfers between devices with their start and end apart: 8 -> 10, of which waited for: 6 -> 7; matrix products, arithmetic and copies ran while one was open for 5% -> 8% of each run, Pallas kernels for 0% -> 0%
where the time goes in v1:
time: 309 us
  waiting for transfers between devices  206 us (67%)
  local copies, waits for them, and re-layouts  30.9 us (10%)
  other arithmetic  20.2 us (7%)
  matrix products  18.9 us (6%)
  starting transfers between devices  18.8 us (6%)
  between operations  14.1 us (5%)
    reduce_scatter x1, waiting for transfers between devices, body(): lax.psum_scatter(lax.dot_general(columns, grad_pre, (((0,), (0,)), ((), (...  82.9 us
    reduce_scatter x1, waiting for transfers between devices, body(): lax.psum_scatter(jnp.concatenate([key_part.reshape(lax.axis_size('seq') *...  64.3 us
    ppermute x3, waiting for transfers between devices, doubled(): other = lax.ppermute(pieces, axis, [(i, i ^ bit) for i in range(devices)])  53.6 us
    ppermute x2, starting transfers between devices, extended(): before = lax.ppermute(last, axis, up)  8.55 us
    ppermute x3, starting transfers between devices, doubled(): other = lax.ppermute(pieces, axis, [(i, i ^ bit) for i in range(devices)])  7.39 us
  transfers between devices with their start and end apart: 10, of which 7 were waited for; matrix products, arithmetic and copies ran while one was open for 8% of the time, Pallas kernels for 0%

profile of v1, /device:TPU:0, one launch (start us, length us, event | category | flops | bytes accessed | tf_op | source)
XLA Modules:
  0.0 308.5 jit_solution(8900866746862414155)
XLA Ops:
  7.2 3.1 collective-permute-start
  10.3 5.1 %collective-permute-done = bf16[1,1,128,768]{3,2,1,0:T(8,128)(2,1)S(1)} collective-permute-done((bf16[1,1,128,768]{3,2,1,0:T(8,128)(2,1)}, bf16[1,1,128,768]{3,2,1,0:T(8,128)(2,1)S(1)}, u32[]{:S(2)}, u32[]{:S(2)}) %collective-permute-start) | collective-permute-done | bytes 196640 | tf_op jit(solution)/shard_map/ppermute | solution.py:26
  15.4 1.0 pad_maximum_fusion.5
  16.4 0.8 fusion.21
  17.2 1.8 collective-permute-start.1
  19.0 1.7 copy.25
  20.7 0.0 reduce-scatter.3.cloned.1.call-start
  20.8 7.1 %collective-permute-done.1 = bf16[2,1,128,768]{3,2,0,1:T(8,128)(2,1)} collective-permute-done((bf16[2,1,128,768]{3,2,0,1:T(8,128)(2,1)}, bf16[2,1,128,768]{3,2,0,1:T(8,128)(2,1)}, u32[]{:S(2)}, u32[]{:S(2)}) %collective-permute-start.1) | collective-permute-done | bytes 393248 | tf_op jit(solution)/shard_map/ppermute | solution.py:26
  27.8 1.1 pad_maximum_fusion.2
  28.9 1.0 reverse_select_fusion.1
  29.9 2.5 collective-permute-start.2
  32.5 0.1 copy.35
  32.6 41.4 %collective-permute-done.2 = bf16[4,1,128,768]{3,2,0,1:T(8,128)(2,1)} collective-permute-done((bf16[4,1,128,768]{3,2,0,1:T(8,128)(2,1)}, bf16[4,1,128,768]{3,2,0,1:T(8,128)(2,1)}, u32[]{:S(2)}, u32[]{:S(2)}) %collective-permute-start.2) | collective-permute-done | bytes 786464 | tf_op jit(solution)/shard_map/ppermute | solution.py:26
  74.0 1.5 pad_maximum_fusion.1
  75.5 1.4 reverse_select_fusion
  77.0 3.8 %copy.24 = bf16[2,4,1,128,768]{3,1,0,4,2:T(4,128)(2,1)} copy(bf16[2,4,1,128,768]{4,3,1,2,0:T(8,128)(2,1)} %reverse_select_fusion) | data formatting | bytes 3145728 | tf_op jit(solution)/shard_map/jit(_where)/select_n | solution.py:29
  80.8 3.8 %reshape_squeeze_reshape_transpose_reshape.3 = bf16[1024,4,192]{0,2,1:T(8,128)(2,1)} reshape(bf16[2,4,1,128,768]{3,1,0,4,2:T(4,128)(2,1)} %copy.24) | data formatting | bytes 3145728 | tf_op jit(solution)/shard_map/reshape;squeeze;reshape;transpose;reshape | solution.py:73
  84.6 1.9 multiply_reduce_fusion
  86.5 0.5 exponential_reduce_fusion
  87.0 0.7 fusion.2
  87.8 0.1 copy-done.1
  87.8 0.9 copy.28
  88.7 1.0 convert_add_fusion.1
  89.8 1.2 broadcast_in_dim.29
  90.9 2.6 reshape.101
  93.5 2.6 broadcast_in_dim.30
  96.1 1.3 fusion.6
  97.4 1.3 multiply_convert_fusion.2
  98.7 3.8 %collective-permute-start.3 = (bf16[2,768]{1,0:T(2,128)(2,1)S(1)}, bf16[2,768]{1,0:T(2,128)(2,1)S(1)}, u32[]{:S(2)}, u32[]{:S(2)}) collective-permute-start(bf16[2,768]{1,0:T(2,128)(2,1)S(1)} %get-tuple-element.26), channel_id=1, source_target_pairs={{0,2},{2,4},{4,6},{6,8},{8,10},{10,12},{12,14},{1,3},{3,5},{5,7},{... | collective-permute-start | bytes 9224 | tf_op jit(solution)/shard_map/ppermute | solution.py:44
  102.6 1.3 collective-permute-start.4
  103.9 0.1 fusion.10
  104.0 0.1 fusion.18
  104.1 3.9 %collective-permute-done.4 = bf16[2,768]{1,0:T(2,128)(2,1)S(1)} collective-permute-done((bf16[2,768]{1,0:T(2,128)(2,1)S(1)}, bf16[2,768]{1,0:T(2,128)(2,1)S(1)}, u32[]{:S(2)}, u32[]{:S(2)}) %collective-permute-start.4) | collective-permute-done | bytes 3104 | tf_op jit(solution)/shard_map/ppermute | solution.py:45
  108.1 0.1 fusion.8
  108.2 0.1 fusion.17
  108.3 2.0 fusion.16
  110.3 1.4 collective-permute-start.5
  111.8 4.7 %collective-permute-start.6 = (bf16[2,384]{1,0:T(2,128)(2,1)S(1)}, bf16[2,384]{1,0:T(2,128)(2,1)S(1)}, u32[]{:S(2)}, u32[]{:S(2)}) collective-permute-start(bf16[2,384]{1,0:T(2,128)(2,1)S(1)} %get-tuple-element.29), channel_id=1, source_target_pairs={{0,2},{2,4},{4,6},{6,8},{8,10},{10,12},{12,14},{1,3},{3,5},{5,7},{... | collective-permute-start | bytes 4616 | tf_op jit(solution)/shard_map/ppermute | solution.py:44
  116.5 0.1 fusion.27
  116.6 0.1 fusion.32
  116.7 0.9 collective-permute-done.6
  117.6 0.1 fusion.24
  117.7 0.1 fusion.30
  117.7 1.1 multiply_reduce_fusion.1
  118.9 1.3 convert_bitcast_fusion.1
  120.1 2.5 reshape.103
  122.7 2.8 reduce_sum.48
  125.4 1.7 copy.29
  127.2 1.1 fusion.19
  128.3 3.6 %convolution_convert_fusion = bf16[4,192,1024]{2,1,0:T(8,128)(2,1)} fusion(bf16[128,4,192]{0,2,1:T(8,128)(2,1)} %bitcast.104, f32[4,128,1024]{2,1,0:T(8,128)} %copy-done.1, f32[4,128]{1,0:T(4,128)S(1)} %log_add_fusion), kind=kOutput, calls=%fused_computation.9 | convolution fusion | flops 203685888 | bytes 3868672 | tf_op jit(solution)/shard_map/hij,ihd->jhd/dot_general | solution.py:141
  132.0 0.8 multiply_convert_fusion.1
  132.8 1.0 copy-done.6
  133.8 1.4 multiply_convert_fusion
  135.2 2.3 copy.31
  137.5 2.6 copy.32
  140.1 3.4 %pad_maximum_fusion = bf16[1024,1280]{1,0:T(8,128)(2,1)} fusion(bf16[1024,768]{1,0:T(8,128)(2,1)} %copy.32, bf16[1024,512]{1,0:T(8,128)(2,1)} %copy.31), kind=kLoop, calls=%fused_computation.1 | loop fusion | flops 5242880 | bytes 5242880 | tf_op jit(solution)/shard_map/concatenate | solution.py:143
  143.5 0.0 reduce-scatter.5.cloned.1.call-start
  143.6 5.3 %convolution_multiply_fusion = f32[3840,384]{1,0:T(8,128)} fusion(bf16[256,3840]{1,0:T(8,128)(2,1)} %copy-done.8, bf16[256,384]{1,0:T(8,128)(2,1)S(1)} %get-tuple-element.23), kind=kOutput, calls=%fused_computation | convolution fusion | flops 756449280 | bytes 8060928 | tf_op jit(solution)/shard_map/dot_general | solution.py:102
  148.9 2.0 fusion.3
  150.9 0.8 copy.33
  151.7 64.3 %reduce-scatter.3.cloned.1.call-done = bf16[128,1280]{1,0:T(8,128)(2,1)} async-done(((bf16[1024,1280]{1,0:T(8,128)(2,1)}), bf16[128,1280]{1,0:T(8,128)(2,1)}) %reduce-scatter.3.cloned.1.call-update) | async-done | bytes 327696 | tf_op jit(solution)/shard_map/reduce_scatter | solution.py:142
  216.0 1.6 slice_bitcast_fusion.1
  217.5 1.6 slice_bitcast_fusion
  219.1 82.9 %reduce-scatter.5.cloned.1.call-done = f32[240,384]{1,0:T(8,128)} async-done(((f32[3840,384]{1,0:T(8,128)}), f32[240,384]{1,0:T(8,128)}) %reduce-scatter.5.cloned.1.call-update) | async-done | bytes 368656 | tf_op jit(solution)/shard_map/reduce_scatter | solution.py:101
  (49 shorter events, 0.3 us)
Async XLA Ops:
  7.2 101.1 %copy-start = (bf16[3840,384]{1,0:T(8,128)(2,1)S(1)}, bf16[3840,384]{1,0:T(8,128)(2,1)}, u32[]{:S(2)}) copy-start(bf16[3840,384]{1,0:T(8,128)(2,1)} %param.14) | copy-start | bytes 8847364
  7.2 77.4 %all-gather.2.cloned.1.call-start = ((), (), s32[]{:S(2)}) async-start(), calls=%async_computation.2 | async-start | bytes 1179648 | tf_op jit(solution)/shard_map/all_gather | solution.py:69
  7.2 8.2 %collective-permute-start = (bf16[1,1,128,768]{3,2,1,0:T(8,128)(2,1)}, bf16[1,1,128,768]{3,2,1,0:T(8,128)(2,1)S(1)}, u32[]{:S(2)}, u32[]{:S(2)}) collective-permute-start(bf16[1,1,128,768]{3,2,1,0:T(8,128)(2,1)} %bitcast.110), channel_id=1, source_target_pairs={{0,2},{2,0},{4,6},{6,4},{8,10},{10,8},{12,14},{14,12},{1,3},{3,1},... | collective-permute-start | bytes 589832 | tf_op jit(solution)/shard_map/ppermute | solution.py:26
  16.4 16.1 %copy-start.16 = (bf16[768]{0:T(1024)(128)(2,1)S(1)}, bf16[768]{0:T(1024)(128)(2,1)}, u32[]{:S(2)}) copy-start(bf16[768]{0:T(1024)(128)(2,1)} %param.13) | copy-start | bytes 4612
  16.4 16.1 %copy-start.15 = (bf16[1,128,512]{2,1,0:T(8,128)(2,1)S(1)}, bf16[1,128,512]{2,1,0:T(8,128)(2,1)}, u32[]{:S(2)}) copy-start(bf16[1,128,512]{2,1,0:T(8,128)(2,1)} %param.8) | copy-start | bytes 393220
  17.2 10.6 %collective-permute-start.1 = (bf16[2,1,128,768]{3,2,0,1:T(8,128)(2,1)}, bf16[2,1,128,768]{3,2,0,1:T(8,128)(2,1)}, u32[]{:S(2)}, u32[]{:S(2)}) collective-permute-start(bf16[2,1,128,768]{3,2,0,1:T(8,128)(2,1)} %get-tuple-element.28), channel_id=1, source_target_pairs={{0,4},{2,6},{4,0},{6,2},{8,12},{10,14},{12,8},{14,10},{1,5},{3,7},... | collective-permute-start | bytes 1179656 | tf_op jit(solution)/shard_map/ppermute | solution.py:26
  20.7 195.3 %reduce-scatter.3.cloned.1.call-start = ((), (), s32[]{:S(2)}) async-start(), calls=%async_computation.3 | async-start | bytes 2949120 | tf_op jit(solution)/shard_map/reduce_scatter | solution.py:142
  29.9 44.1 %collective-permute-start.2 = (bf16[4,1,128,768]{3,2,0,1:T(8,128)(2,1)}, bf16[4,1,128,768]{3,2,0,1:T(8,128)(2,1)}, u32[]{:S(2)}, u32[]{:S(2)}) collective-permute-start(bf16[4,1,128,768]{3,2,0,1:T(8,128)(2,1)} %bitcast.8), channel_id=1, source_target_pairs={{0,8},{2,10},{4,12},{6,14},{8,0},{10,2},{12,4},{14,6},{1,9},{3,11}... | collective-permute-start | bytes 2359304 | tf_op jit(solution)/shard_map/ppermute | solution.py:26
  32.6 52.0 %copy-start.12 = (bf16[1,128,512]{1,2,0:T(8,128)(2,1)}, bf16[1,128,512]{1,2,0:T(8,128)(2,1)S(1)}, u32[]{:S(2)}) copy-start(bf16[1,128,512]{1,2,0:T(8,128)(2,1)S(1)} %copy.35) | copy-start | bytes 393220
  84.6 2.4 copy-start.3
  86.5 1.3 copy-start.1
  87.0 1.7 copy-start.14
  87.8 0.9 copy-start.9
  89.8 6.3 %copy-start.7 = (bf16[1,256,768]{2,1,0:T(8,128)(2,1)S(1)}, bf16[1,256,768]{2,1,0:T(8,128)(2,1)}, u32[]{:S(2)}) copy-start(bf16[1,256,768]{2,1,0:T(8,128)(2,1)} %param.12) | copy-start | bytes 1179652
  98.7 9.6 %copy-start.17 = (bf16[1,256,384]{2,1,0:T(8,128)(2,1)S(1)}, bf16[1,256,384]{2,1,0:T(8,128)(2,1)}, u32[]{:S(2)}) copy-start(bf16[1,256,384]{2,1,0:T(8,128)(2,1)} %param.15) | copy-start | bytes 589828
  98.7 5.1 %collective-permute-start.3 = (bf16[2,768]{1,0:T(2,128)(2,1)S(1)}, bf16[2,768]{1,0:T(2,128)(2,1)S(1)}, u32[]{:S(2)}, u32[]{:S(2)}) collective-permute-start(bf16[2,768]{1,0:T(2,128)(2,1)S(1)} %get-tuple-element.26), channel_id=1, source_target_pairs={{0,2},{2,4},{4,6},{6,8},{8,10},{10,12},{12,14},{1,3},{3,5},{5,7},{... | collective-permute-start | bytes 9224 | tf_op jit(solution)/shard_map/ppermute | solution.py:44
  102.6 5.5 %collective-permute-start.4 = (bf16[2,768]{1,0:T(2,128)(2,1)S(1)}, bf16[2,768]{1,0:T(2,128)(2,1)S(1)}, u32[]{:S(2)}, u32[]{:S(2)}) collective-permute-start(bf16[2,768]{1,0:T(2,128)(2,1)S(1)} %get-tuple-element.25), channel_id=1, source_target_pairs={{2,0},{4,2},{6,4},{8,6},{10,8},{12,10},{14,12},{3,1},{5,3},{7,5},{... | collective-permute-start | bytes 9224 | tf_op jit(solution)/shard_map/ppermute | solution.py:45
  108.3 2.0 copy-start.8
  110.3 7.4 %copy-start.5 = (f32[256,768]{1,0:T(8,128)S(1)}, f32[256,768]{1,0:T(8,128)}, u32[]{:S(2)}) copy-start(f32[256,768]{1,0:T(8,128)} %reshape.101) | copy-start | bytes 2359300
  110.3 6.2 %collective-permute-start.5 = (bf16[2,384]{1,0:T(2,128)(2,1)S(1)}, bf16[2,384]{1,0:T(2,128)(2,1)S(1)}, u32[]{:S(2)}, u32[]{:S(2)}) collective-permute-start(bf16[2,384]{1,0:T(2,128)(2,1)S(1)} %get-tuple-element.30), channel_id=1, source_target_pairs={{2,0},{4,2},{6,4},{8,6},{10,8},{12,10},{14,12},{3,1},{5,3},{7,5},{... | collective-permute-start | bytes 4616 | tf_op jit(solution)/shard_map/ppermute | solution.py:45
  111.8 5.8 %collective-permute-start.6 = (bf16[2,384]{1,0:T(2,128)(2,1)S(1)}, bf16[2,384]{1,0:T(2,128)(2,1)S(1)}, u32[]{:S(2)}, u32[]{:S(2)}) collective-permute-start(bf16[2,384]{1,0:T(2,128)(2,1)S(1)} %get-tuple-element.29), channel_id=1, source_target_pairs={{0,2},{2,4},{4,6},{6,8},{8,10},{10,12},{12,14},{1,3},{3,5},{5,7},{... | collective-permute-start | bytes 4616 | tf_op jit(solution)/shard_map/ppermute | solution.py:44
  120.1 7.0 %copy-start.10 = (f32[4,192,128]{2,1,0:T(8,128)S(1)}, f32[4,192,128]{2,1,0:T(8,128)}, u32[]{:S(2)}) copy-start(f32[4,192,128]{2,1,0:T(8,128)} %copy-done.9) | copy-start | bytes 1179652
  127.2 4.8 %copy-start.2 = (f32[4,128,1024]{2,1,0:T(8,128)S(1)}, f32[4,128,1024]{2,1,0:T(8,128)}, u32[]{:S(2)}) copy-start(f32[4,128,1024]{2,1,0:T(8,128)} %copy-done.1) | copy-start | bytes 6291460
  127.2 4.8 %copy-start.4 = (bf16[1024,4,192]{0,2,1:T(8,128)(2,1)S(1)}, bf16[1024,4,192]{0,2,1:T(8,128)(2,1)}, u32[]{:S(2)}) copy-start(bf16[1024,4,192]{0,2,1:T(8,128)(2,1)} %reshape_squeeze_reshape_transpose_reshape.3) | copy-start | bytes 4718596
  127.2 4.8 %copy-start.11 = (bf16[128,768]{0,1:T(8,128)(2,1)S(1)}, bf16[128,768]{0,1:T(8,128)(2,1)}, u32[]{:S(2)}) copy-start(bf16[128,768]{0,1:T(8,128)(2,1)} %copy.29) | copy-start | bytes 589828
  132.0 1.8 copy-start.13
  132.8 1.0 copy-start.6
  143.5 158.5 %reduce-scatter.5.cloned.1.call-start = ((), (), s32[]{:S(2)}) async-start(), calls=%async_computation.4 | async-start | bytes 6266880 | tf_op jit(solution)/shard_map/reduce_scatter | solution.py:101
Sparse Core Ops, SparseCore 0:
  20.8 62.1 all-gather.1
  143.7 72.2 reduce-scatter.2
  220.5 81.4 reduce-scatter.4
